TPU v7x, 32 devices: a whole 2x2x4 slice. The times are simulated.
32 devices in a mesh: led: 4 (over y, x), row: 8 (over z, core).
Axes of the slice: x: 2, y: 2, z: 4, core: 2. Of those that a mesh axis runs over, the one named last changes fastest.
Arguments:
- spectrum: float32 [2, 4096, 4096], P(None, 'led', 'row'), may hold values from -6 to 6
- amplitudes: float32 [4, 2048, 2048], P('led', 'row'), may hold values from 0.2 to 3
- offsets: int32 [4, 2], replicated, may hold values from 0 to 2048
- coeffs: float32 [6], replicated, may hold values from -2.5 to 2.5
Outputs:
- updated: float32 [2, 4096, 4096], P(None, 'led', 'row')
All inputs are finite; a program needn't handle non-finite values.
Results may differ from a plain program's by a relative error of at most 0.0001.
Values sent between devices are 32-bit elements; how exact they have to be, the bound alone decides.
No kernel may reach another device: no remote copies, remote signals or barrier semaphores. Data moves between devices by JAX's collectives and lax.ppermute only.
A program may use at most 128 MiB of HBM per device.

v0:
```python
import math
import jax
import jax.numpy as jnp
from jax import lax
from jax.sharding import PartitionSpec as P

SOFTENING = 0.1
HIGHEST_PRECISION = lax.Precision.HIGHEST


def pupil_at(down_index, across_index, coeffs, centre):
    offset_down = down_index - centre
    offset_across = across_index - centre
    inside = offset_down * offset_down + offset_across * offset_across < centre * centre
    upper_norm = offset_down.astype(jnp.float32) * (1.0 / centre)
    lateral = offset_across.astype(jnp.float32) * (1.0 / centre)
    radial = upper_norm * upper_norm + lateral * lateral
    phases = (
        coeffs[0] * (2.0 * radial - 1.0)
        + coeffs[1] * (upper_norm * upper_norm - lateral * lateral)
        + coeffs[2] * (2.0 * upper_norm * lateral)
        + (3.0 * radial - 2.0) * (coeffs[3] * upper_norm + coeffs[4] * lateral)
        + coeffs[5] * (6.0 * radial * radial - 6.0 * radial + 1.0)
    )
    weight = jnp.where(inside, 1.0, 0.0).astype(jnp.float32)
    return (weight * jnp.cos(phases), weight * jnp.sin(phases))


def tables(outer_size, inner_size, direction):
    length = outer_size * inner_size
    angle_step = direction * 2.0 * math.pi / length
    first_index = jnp.arange(outer_size, dtype=jnp.int32)
    grid_first = first_index[:, None] * first_index[None, :] * inner_size % length
    angles_first = grid_first.astype(jnp.float32) * angle_step
    index_k = jnp.arange(outer_size, dtype=jnp.int32)[:, None, None]
    index_r = jnp.arange(inner_size, dtype=jnp.int32)[None, :, None]
    index_j = jnp.arange(inner_size, dtype=jnp.int32)[None, None, :]
    grid_second = index_r * (index_k + outer_size * index_j) % length
    angles_second = grid_second.astype(jnp.float32) * angle_step
    return (
        jnp.cos(angles_first),
        jnp.sin(angles_first),
        jnp.cos(angles_second),
        jnp.sin(angles_second),
    )


def transform(paired, inputs, middle, output, outer_size, inner_size, direction):
    first_re, first_im, second_re, second_im = tables(outer_size, inner_size, direction)
    scaling = 1.0 / math.sqrt(outer_size * inner_size)
    first_table = jnp.stack([jnp.stack([first_re, first_im]), jnp.stack([-first_im, first_re])])
    second_table = (
        jnp.stack([jnp.stack([second_re, second_im]), jnp.stack([-second_im, second_re])]) * scaling
    )
    middle_pair = jnp.einsum(
        "p" + inputs + ",pqtk->q" + middle, paired, first_table, precision=HIGHEST_PRECISION
    )
    return jnp.einsum(
        "p" + middle + ",pqkrj->q" + output, middle_pair, second_table, precision=HIGHEST_PRECISION
    )


def correct(field_re, field_im, measured):
    magnitude = jnp.sqrt(field_re * field_re + field_im * field_im + SOFTENING)
    factor = measured / magnitude
    return (field_re * factor - field_re, field_im * factor - field_im)


def on_device(spectrum, amplitudes, offsets, coeffs):
    led_count = lax.axis_size("led")
    row_count = lax.axis_size("row")
    led_index = lax.axis_index("led")
    row_index = lax.axis_index("row")
    size_rows = spectrum.shape[1]
    size_cols = spectrum.shape[2]
    window = amplitudes.shape[2]
    centre = window // 2
    block_rows = window // row_count
    outer_rows = window // led_count
    outer_cols = window // row_count
    row_shift = offsets[led_index, 0]
    col_shift = offsets[led_index, 1]
    measured = amplitudes[0]
    shape_cols = (2, block_rows, outer_cols, row_count)
    region = lax.all_gather(spectrum, "led", axis=1, tiled=True)
    band_rows = lax.dynamic_slice_in_dim(region, row_shift, window, 1)
    row_ids = jnp.arange(window, dtype=jnp.int32)[:, None]
    col_ids = (row_index * size_cols + jnp.arange(size_cols, dtype=jnp.int32))[None, :] - col_shift
    pupil_re, pupil_im = pupil_at(row_ids, col_ids, coeffs, centre)
    lit_re = pupil_re * band_rows[0] - pupil_im * band_rows[1]
    lit_im = pupil_re * band_rows[1] + pupil_im * band_rows[0]
    shape_rows = (2, outer_rows, led_count, size_cols)
    half = transform(
        jnp.stack([lit_re, lit_im]).reshape(shape_rows),
        "trc",
        "krc",
        "jkc",
        outer_rows,
        led_count,
        1.0,
    )
    stacked = half.reshape(2, window, size_cols)
    spread = lax.all_to_all(stacked, "row", split_axis=1, concat_axis=2, tiled=True)
    window_part = lax.dynamic_slice_in_dim(spread, col_shift, window, 2)
    field = transform(
        window_part.reshape(shape_cols), "ytr", "ykr", "yjk", outer_cols, row_count, 1.0
    )
    field = field.reshape(2, block_rows, window)
    diff_re, diff_im = correct(field[0], field[1], measured)
    back = transform(
        jnp.stack([diff_re, diff_im]).reshape(shape_cols),
        "ytr",
        "ykr",
        "yjk",
        outer_cols,
        row_count,
        -1.0,
    )
    padded = jnp.zeros((2, block_rows, row_count * size_cols), jnp.float32)
    padded = lax.dynamic_update_slice_in_dim(
        padded, back.reshape(2, block_rows, window), col_shift, 2
    )
    gathered_cols = lax.all_to_all(padded, "row", split_axis=2, concat_axis=1, tiled=True)
    spec = transform(
        gathered_cols.reshape(shape_rows), "trc", "krc", "jkc", outer_rows, led_count, -1.0
    ).reshape(2, window, size_cols)
    upd_re = pupil_re * spec[0] + pupil_im * spec[1]
    upd_im = pupil_re * spec[1] - pupil_im * spec[0]
    embedded = jnp.zeros((2, size_rows * led_count, size_cols), jnp.float32)
    embedded = lax.dynamic_update_slice_in_dim(embedded, jnp.stack([upd_re, upd_im]), row_shift, 1)
    summed = lax.psum_scatter(embedded, "led", scatter_dimension=1, tiled=True)
    return spectrum + summed


def solution(mesh):
    return jax.shard_map(
        on_device,
        mesh=mesh,
        in_specs=(P(None, "led", "row"), P("led", "row", None), P(), P()),
        out_specs=P(None, "led", "row"),
        check_vma=False,
    )
```

profile of v0, /device:TPU:0, one launch (start us, length us, event | category | flops | bytes accessed | tf_op | source)
XLA Modules:
  0.0 1087.1 jit_solution(2746678404710610124)
XLA Ops:
  27.8 141.4 %all-gather.2.cloned.1.call-done = f32[2,4096,512]{2,1,0:T(8,128)} async-done(((f32[2,1024,512]{2,1,0:T(8,128)}), f32[2,4096,512]{2,1,0:T(8,128)}) %all-gather.2.cloned.1.call-update) | async-done | bytes 16777232 | tf_op jit(solution)/shard_map/all_gather | solution.py:85
  169.3 26.9 %multiply_subtract_fusion = (f32[1,2048,512]{2,1,0:T(8,128)}, f32[1,2048,512]{2,1,0:T(8,128)}) fusion(f32[2,4096,512]{2,1,0:T(8,128)} %all-gather.2.cloned.1.call-done, s32[]{:T(128)S(6)} %select_n.238, s32[]{:T(128)S(6)} %add.718, f32[]{:T(128)} %bitcast.6, f32[512]{0:T(512)S(1)} %get-tuple-element.53, f32[2048]{0:T(1024)S(1)} %get-tuple-element.58, ...), kind=kLoop, calls=%fused_computation.55 | loop fusion | flops 33554432 | bytes 16818200 | tf_op jit(solution)/shard_map/sub | solution.py:90
  196.1 7.9 stack.215
  209.6 7.7 stack.216
  221.4 28.3 %fusion.46 = f32[2,512,4,512,1]{3,1,2,0,4:T(8,128)} fusion(f32[1,512,4,512]{3,1,0,2:T(8,128)S(1)} %copy.144, f32[1,512,4,512]{3,1,0,2:T(8,128)S(1)} %copy-done.3, f32[1,2,512,512]{2,3,0,1:T(8,128)S(1)} %copy-done.4, f32[1,2,512,512]{2,3,0,1:T(8,128)S(1)} %get-tuple-element.17), kind=kOutput, calls=%fused_computation.58 | convolution fusion | flops 25772949504 | bytes 20971520 | tf_op jit(solution)/shard_map/ptrc,pqtk->qkrc/dot_general | solution.py:55
  249.7 32.7 %fusion.11 = f32[2,4,512,512]{3,1,0,2:T(4,128)S(1)} fusion(f32[2,2,512,4,4]{3,4,0,1,2:T(4,128)} %copy.145, f32[2,512,4,512,1]{3,1,2,0,4:T(8,128)} %fusion.46), kind=kOutput, calls=%fused_computation.19 | convolution fusion | flops 201326592 | bytes 16908288 | tf_op jit(solution)/shard_map/pkrc,pqkrj->qjkc/dot_general | solution.py:58
  287.2 16.5 %copy.148 = f32[2,2048,512]{2,0,1:T(2,128)} copy(f32[2,2048,512]{2,1,0:T(8,128)S(1)} %bitcast.186) | data formatting | bytes 16777216 | tf_op jit(solution)/shard_map/reshape | solution.py:102
  327.6 165.1 %all-to-all-done = f32[2,2048,512]{2,0,1:T(2,128)} async-done(((f32[2,2048,512]{2,0,1:T(2,128)}), f32[2,2048,512]{2,0,1:T(2,128)}, u32[]{:S(2)}, u32[]{:S(2)}) %all-to-all-start) | async-done | bytes 8388640 | tf_op jit(solution)/shard_map/all_to_all | solution.py:103
  492.7 8.2 copy.149
  501.0 8.8 copy.150
  519.5 9.7 fusion.54
  529.3 7.0 fusion.47
  545.6 9.1 fusion.53
  554.8 7.0 fusion.50
  569.6 12.4 %copy_dynamic-update-slice_fusion = f32[2,256,4096]{1,0,2:T(2,128)} fusion(f32[2,256,4096]{1,0,2:T(2,128)} %broadcast_in_dim.15, s32[]{:T(128)S(6)} %select_n.239, f32[2,256,2048]{1,2,0:T(8,128)S(1)} %bitcast.190), kind=kLoop, calls=%fused_computation.52 | loop fusion | bytes 8388612 | tf_op jit(solution)/shard_map/dynamic_update_slice | solution.py:120
  600.4 170.5 %all-to-all-done.1 = f32[2,256,4096]{1,0,2:T(2,128)} async-done(((f32[2,256,4096]{1,0,2:T(2,128)}), f32[2,256,4096]{1,0,2:T(2,128)}, u32[]{:S(2)}, u32[]{:S(2)}) %all-to-all-start.1) | async-done | bytes 8388640 | tf_op jit(solution)/shard_map/all_to_all | solution.py:123
  770.9 7.3 copy.164
  778.2 13.3 %copy.165 = f32[2,8,256,512]{3,0,2,1:T(2,128)} copy(f32[2,8,256,512]{2,3,1,0:T(8,128)} %bitcast.188) | data formatting | bytes 16777216 | tf_op jit(solution)/shard_map/all_to_all | solution.py:123
  791.5 31.6 %fusion.41 = f32[2,512,4,512,1]{3,1,2,0,4:T(8,128)} fusion(f32[2,512,4,512]{3,0,2,1:T(2,128)} %bitcast.191, f32[1,2,512,512]{2,3,1,0:T(8,128)} %get-tuple-element.16, f32[1,2,512,512]{2,3,1,0:T(8,128)S(1)} %get-tuple-element.15), kind=kOutput, calls=%fused_computation.57 | convolution fusion | flops 25770852352 | bytes 20971520 | tf_op jit(solution)/shard_map/ptrc,pqtk->qkrc/dot_general | solution.py:55
  823.2 32.4 %fusion.14 = f32[2,4,512,512]{3,1,0,2:T(4,128)S(1)} fusion(f32[2,2,512,4,4]{3,4,0,1,2:T(4,128)} %copy.168, f32[2,512,4,512,1]{3,1,2,0,4:T(8,128)} %fusion.41), kind=kOutput, calls=%fused_computation.20 | convolution fusion | flops 201326592 | bytes 16908288 | tf_op jit(solution)/shard_map/pkrc,pqkrj->qjkc/dot_general | solution.py:58
  863.9 23.1 %fusion.32 = (f32[1,2048,512]{2,1,0:T(8,128)S(1)}, f32[1,2048,512]{2,1,0:T(8,128)S(1)}) fusion(f32[1,4,512,512]{3,2,1,0:T(8,128)S(1)} %copy.171, f32[1,4,512,512]{3,2,1,0:T(8,128)S(1)} %copy.170, f32[]{:T(128)} %bitcast.6, f32[512]{0:T(512)S(1)} %get-tuple-element.53, f32[2048]{0:T(1024)S(1)} %get-tuple-element.58, f32[512]{0:T(512)S(1)} %get-tuple-element.54, ...), kind=kLoop, calls=%fused_computation.41 | loop fusion | flops 33554432 | bytes 16818192 | tf_op jit(solution)/shard_map/add | solution.py:127
  891.3 7.9 broadcast_in_dim.12
  899.2 22.7 %dynamic_update_slice.7 = f32[2,4096,512]{2,1,0:T(8,128)} dynamic-update-slice(f32[2,4096,512]{2,1,0:T(8,128)} %broadcast_in_dim.12, f32[2,2048,512]{2,1,0:T(8,128)} %pad_maximum_fusion, s32[]{:T(128)} %constant.100.clone.1, s32[]{:T(128)S(6)} %select_n.238, s32[]{:T(128)} %constant.100.clone.1) | dynamic-update-slice | bytes 16777220 | tf_op jit(solution)/shard_map/dynamic_update_slice | solution.py:130
  921.8 151.7 %reduce-scatter.2.cloned.1.call-done = f32[2,1024,512]{2,1,0:T(8,128)} async-done(((f32[2,4096,512]{2,1,0:T(8,128)}), f32[2,1024,512]{2,1,0:T(8,128)}) %reduce-scatter.2.cloned.1.call-update) | async-done | bytes 4194320 | tf_op jit(solution)/shard_map/reduce_scatter | solution.py:131
  (75 shorter events, 118.4 us)
Async XLA Ops:
  6.5 0.7 copy-start.6
  6.5 2.8 copy-start.5
  6.5 162.7 %all-gather.2.cloned.1.call-start = ((), (), s32[]{:S(2)}) async-start(), calls=%async_computation.3 | async-start | bytes 20971520 | tf_op jit(solution)/shard_map/all_gather | solution.py:85
  217.3 3.7 copy-start.3
  217.3 4.1 copy-start.4
  303.7 189.0 %all-to-all-start = ((f32[2,2048,512]{2,0,1:T(2,128)}), f32[2,2048,512]{2,0,1:T(2,128)}, u32[]{:S(2)}, u32[]{:S(2)}) async-start(f32[2,2048,512]{2,0,1:T(2,128)} %copy.148), calls=%async_computation | async-start | bytes 16777216 | tf_op jit(solution)/shard_map/all_to_all | solution.py:103
  519.5 9.7 copy-start.1
  540.8 3.1 copy-start.2
  545.6 9.1 copy-start
  582.1 188.8 %all-to-all-start.1 = ((f32[2,256,4096]{1,0,2:T(2,128)}), f32[2,256,4096]{1,0,2:T(2,128)}, u32[]{:S(2)}, u32[]{:S(2)}) async-start(f32[2,256,4096]{1,0,2:T(2,128)} %copy_dynamic-update-slice_fusion), calls=%async_computation.1 | async-start | bytes 16777216 | tf_op jit(solution)/shard_map/all_to_all | solution.py:123
  587.0 486.5 %reduce-scatter.2.cloned.1.call-start = ((), (), s32[]{:S(2)}) async-start(), calls=%async_computation.4 | async-start | bytes 20971520 | tf_op jit(solution)/shard_map/reduce_scatter | solution.py:131
Sparse Core Ops, SparseCore 0:
  9.2 160.0 all-gather.1
  922.0 151.5 reduce-scatter.1
where the time goes:
time: 1100 us; the launch traced here: 1090 us
  waiting for transfers between devices  630 us (57%)
  local copies, waits for them, and re-layouts  178 us (16%)
  matrix products  158 us (14%)
  other arithmetic  91.9 us (8%)
  between operations  19.3 us (2%)
    all_to_all x1, waiting for transfers between devices, on_device(): lax.all_to_all(padded, 'row', split_axis=2, concat_axis=1, tiled=True)  171 us
    all_to_all x1, waiting for transfers between devices, on_device(): lax.all_to_all(stacked, 'row', split_axis=1, concat_axis=2, tiled=True)  165 us
    reduce_scatter x1, waiting for transfers between devices, on_device(): summed = lax.psum_scatter(embedded, 'led', scatter_dimension=1, tiled=True)  152 us
    all_gather x1, waiting for transfers between devices, on_device(): region = lax.all_gather(spectrum, 'led', axis=1, tiled=True)  141 us
    dot_general x4, matrix products, transform(): jnp.einsum('p' + middle + ',pqkrj->q' + output, middle_pair, second_table...  79.1 us
    dot_general x4, matrix products, transform(): jnp.einsum('p' + inputs + ',pqtk->q' + middle, paired, first_table, preci...  78.8 us
    sub x1, other arithmetic, on_device(): lit_re = pupil_re * band_rows[0] - pupil_im * band_rows[1]  26.9 us
    another operation x4, local copies, waits for them, and re-layouts, on_device(): jnp.stack([lit_re, lit_im]).reshape(shape_rows)  24.9 us
  transfers between devices with their start and end apart: 4, of which 4 were waited for; matrix products, arithmetic and copies ran while one was open for 4% of the time, Pallas kernels for 0%

commit v1 on v0

--- a/solution.py
+++ b/solution.py
@@ -6,6 +6,27 @@
 
 SOFTENING = 0.1
 HIGHEST_PRECISION = lax.Precision.HIGHEST
+
+
+def laid_out(tiles, dim):
+    shape = list(tiles.shape[1:])
+    shape[dim] *= tiles.shape[0]
+    return jnp.moveaxis(tiles, 0, dim).reshape(shape)
+
+
+def doubled(array, axis):
+    count, mine = (lax.axis_size(axis), lax.axis_index(axis))
+    blocks, bit = (array[None], 1)
+    while bit < count:
+        theirs = lax.ppermute(blocks, axis, [(i, i ^ bit) for i in range(count)])
+        low = mine & bit == 0
+        blocks = jnp.concatenate([jnp.where(low, blocks, theirs), jnp.where(low, theirs, blocks)])
+        bit *= 2
+    return blocks
+
+
+def gather_by_bits(x, axis, dim):
+    return laid_out(doubled(x, axis), dim)
 
 
 def pupil_at(down_index, across_index, coeffs, centre):
@@ -82,7 +103,7 @@
     col_shift = offsets[led_index, 1]
     measured = amplitudes[0]
     shape_cols = (2, block_rows, outer_cols, row_count)
-    region = lax.all_gather(spectrum, "led", axis=1, tiled=True)
+    region = gather_by_bits(spectrum, "led", 1)
     band_rows = lax.dynamic_slice_in_dim(region, row_shift, window, 1)
     row_ids = jnp.arange(window, dtype=jnp.int32)[:, None]
     col_ids = (row_index * size_cols + jnp.arange(size_cols, dtype=jnp.int32))[None, :] - col_shift

time: 1100 us -> 1230 us (1.12)
  waiting for transfers between devices: 630 us -> 739 us
  other arithmetic: 91.9 us -> 116 us
    ppermute x0 -> x2, waiting for transfers between devices: none -> 250 us  [doubled(): theirs = lax.ppermute(blocks, axis, [(i, i ^ bit) for i in range(count)])]
    all_gather x1 -> x0, waiting for transfers between devices: 141 us -> none  [on_device(): region = lax.all_gather(spectrum, 'led', axis=1, tiled=True)]
    select_n x0 -> x2, other arithmetic: none -> 13.8 us  [doubled(): jnp.where(low, blocks, theirs)]
  transfers between devices with their start and end apart: 4 -> 5, of which waited for: 4 -> 5; matrix products, arithmetic and copies ran while one was open for 4% -> 4% of each run, Pallas kernels for 0% -> 0%
where the time goes in v1:
time: 1230 us
  waiting for transfers between devices  739 us (60%)
  local copies, waits for them, and re-layouts  182 us (15%)
  matrix products  158 us (13%)
  other arithmetic  116 us (9%)
  between operations  19.1 us (2%)
  starting transfers between devices  14.9 us (1%)
    ppermute x2, waiting for transfers between devices, doubled(): theirs = lax.ppermute(blocks, axis, [(i, i ^ bit) for i in range(count)])  250 us
    all_to_all x1, waiting for transfers between devices, on_device(): lax.all_to_all(padded, 'row', split_axis=2, concat_axis=1, tiled=True)  171 us
    all_to_all x1, waiting for transfers between devices, on_device(): lax.all_to_all(stacked, 'row', split_axis=1, concat_axis=2, tiled=True)  165 us
    reduce_scatter x1, waiting for transfers between devices, on_device(): summed = lax.psum_scatter(embedded, 'led', scatter_dimension=1, tiled=True)  153 us
    dot_general x4, matrix products, transform(): jnp.einsum('p' + middle + ',pqkrj->q' + output, middle_pair, second_table...  79.1 us
    dot_general x4, matrix products, transform(): jnp.einsum('p' + inputs + ',pqtk->q' + middle, paired, first_table, preci...  78.8 us
    sub x1, other arithmetic, on_device(): lit_re = pupil_re * band_rows[0] - pupil_im * band_rows[1]  25.7 us
    another operation x4, local copies, waits for them, and re-layouts, on_device(): jnp.stack([lit_re, lit_im]).reshape(shape_rows)  24.6 us
  transfers between devices with their start and end apart: 5, of which 5 were waited for; matrix products, arithmetic and copies ran while one was open for 4% of the time, Pallas kernels for 0%

profile of v1, /device:TPU:0, one launch (start us, length us, event | category | flops | bytes accessed | tf_op | source)
XLA Modules:
  0.0 1228.4 jit_solution(14226821160376363154)
XLA Ops:
  9.5 90.9 %collective-permute-done = f32[1,2,1024,512]{3,2,1,0:T(8,128)} collective-permute-done((f32[1,2,1024,512]{3,2,1,0:T(8,128)}, f32[1,2,1024,512]{3,2,1,0:T(8,128)}, u32[]{:S(2)}, u32[]{:S(2)}) %collective-permute-start) | collective-permute-done | bytes 4194336 | tf_op jit(solution)/shard_map/ppermute | solution.py:21
  133.2 159.4 %collective-permute-done.1 = f32[2,2,1024,512]{3,2,1,0:T(8,128)} collective-permute-done((f32[2,2,1024,512]{3,2,1,0:T(8,128)}, f32[2,2,1024,512]{3,2,1,0:T(8,128)}, u32[]{:S(2)}, u32[]{:S(2)}) %collective-permute-start.1) | collective-permute-done | bytes 8388640 | tf_op jit(solution)/shard_map/ppermute | solution.py:21
  292.6 9.3 broadcast_select_fusion.1
  310.9 25.7 %multiply_subtract_fusion = (f32[1,2048,512]{2,1,0:T(8,128)}, f32[1,2048,512]{2,1,0:T(8,128)}) fusion(f32[2,4096,512]{2,1,0:T(8,128)S(1)} %bitcast.192, s32[]{:T(128)S(6)} %select_n.268, s32[]{:T(128)S(6)} %add.718, f32[]{:T(128)} %bitcast.6, f32[512]{0:T(512)S(1)} %get-tuple-element.57, f32[2048]{0:T(1024)S(1)} %get-tuple-element.62, ...), kind=kLoop, calls=%fused_computation.57 | loop fusion | flops 33554432 | bytes 16818200 | tf_op jit(solution)/shard_map/sub | solution.py:111
  336.6 7.7 stack.215
  349.8 7.7 stack.216
  361.6 28.3 %fusion.46 = f32[2,512,4,512,1]{3,1,2,0,4:T(8,128)} fusion(f32[1,512,4,512]{3,1,0,2:T(8,128)S(1)} %copy.151, f32[1,512,4,512]{3,1,0,2:T(8,128)S(1)} %copy-done.7, f32[1,2,512,512]{2,3,0,1:T(8,128)S(1)} %copy-done.8, f32[1,2,512,512]{2,3,0,1:T(8,128)S(1)} %get-tuple-element.21), kind=kOutput, calls=%fused_computation.62 | convolution fusion | flops 25772949504 | bytes 20971520 | tf_op jit(solution)/shard_map/ptrc,pqtk->qkrc/dot_general | solution.py:76
  390.0 32.7 %fusion.11 = f32[2,4,512,512]{3,1,0,2:T(4,128)S(1)} fusion(f32[2,2,512,4,4]{3,4,0,1,2:T(4,128)} %copy.152, f32[2,512,4,512,1]{3,1,2,0,4:T(8,128)} %fusion.46), kind=kOutput, calls=%fused_computation.21 | convolution fusion | flops 201326592 | bytes 16908288 | tf_op jit(solution)/shard_map/pkrc,pqkrj->qjkc/dot_general | solution.py:79
  427.5 16.5 %copy.155 = f32[2,2048,512]{2,0,1:T(2,128)} copy(f32[2,2048,512]{2,1,0:T(8,128)S(1)} %bitcast.193) | data formatting | bytes 16777216 | tf_op jit(solution)/shard_map/reshape | solution.py:123
  467.5 165.5 %all-to-all-done = f32[2,2048,512]{2,0,1:T(2,128)} async-done(((f32[2,2048,512]{2,0,1:T(2,128)}), f32[2,2048,512]{2,0,1:T(2,128)}, u32[]{:S(2)}, u32[]{:S(2)}) %all-to-all-start) | async-done | bytes 8388640 | tf_op jit(solution)/shard_map/all_to_all | solution.py:124
  633.0 8.2 copy.156
  641.2 8.8 copy.157
  659.8 9.7 fusion.54
  685.9 9.1 fusion.53
  709.9 12.4 %copy_dynamic-update-slice_fusion = f32[2,256,4096]{1,0,2:T(2,128)} fusion(f32[2,256,4096]{1,0,2:T(2,128)} %broadcast_in_dim.17, s32[]{:T(128)S(6)} %select_n.269, f32[2,256,2048]{1,2,0:T(8,128)S(1)} %bitcast.198), kind=kLoop, calls=%fused_computation.54 | loop fusion | bytes 8388612 | tf_op jit(solution)/shard_map/dynamic_update_slice | solution.py:141
  740.7 170.5 %all-to-all-done.1 = f32[2,256,4096]{1,0,2:T(2,128)} async-done(((f32[2,256,4096]{1,0,2:T(2,128)}), f32[2,256,4096]{1,0,2:T(2,128)}, u32[]{:S(2)}, u32[]{:S(2)}) %all-to-all-start.1) | async-done | bytes 8388640 | tf_op jit(solution)/shard_map/all_to_all | solution.py:144
  911.2 7.3 copy.171
  918.5 13.3 %copy.172 = f32[2,8,256,512]{3,0,2,1:T(2,128)} copy(f32[2,8,256,512]{2,3,1,0:T(8,128)} %bitcast.195) | data formatting | bytes 16777216 | tf_op jit(solution)/shard_map/all_to_all | solution.py:144
  931.8 31.6 %fusion.41 = f32[2,512,4,512,1]{3,1,2,0,4:T(8,128)} fusion(f32[2,512,4,512]{3,0,2,1:T(2,128)} %bitcast.199, f32[1,2,512,512]{2,3,1,0:T(8,128)} %get-tuple-element.20, f32[1,2,512,512]{2,3,1,0:T(8,128)S(1)} %get-tuple-element.19), kind=kOutput, calls=%fused_computation.61 | convolution fusion | flops 25770852352 | bytes 20971520 | tf_op jit(solution)/shard_map/ptrc,pqtk->qkrc/dot_general | solution.py:76
  963.4 32.4 %fusion.14 = f32[2,4,512,512]{3,1,0,2:T(4,128)S(1)} fusion(f32[2,2,512,4,4]{3,4,0,1,2:T(4,128)} %copy.175, f32[2,512,4,512,1]{3,1,2,0,4:T(8,128)} %fusion.41), kind=kOutput, calls=%fused_computation.22 | convolution fusion | flops 201326592 | bytes 16908288 | tf_op jit(solution)/shard_map/pkrc,pqkrj->qjkc/dot_general | solution.py:79
  1004.2 23.0 %fusion.32 = (f32[1,2048,512]{2,1,0:T(8,128)S(1)}, f32[1,2048,512]{2,1,0:T(8,128)S(1)}) fusion(f32[1,4,512,512]{3,2,1,0:T(8,128)S(1)} %copy.178, f32[1,4,512,512]{3,2,1,0:T(8,128)S(1)} %copy.177, f32[]{:T(128)} %bitcast.6, f32[512]{0:T(512)S(1)} %get-tuple-element.57, f32[2048]{0:T(1024)S(1)} %get-tuple-element.62, f32[512]{0:T(512)S(1)} %get-tuple-element.58, ...), kind=kLoop, calls=%fused_computation.43 | loop fusion | flops 33554432 | bytes 16818192 | tf_op jit(solution)/shard_map/add | solution.py:148
  1031.5 7.9 broadcast_in_dim.14
  1039.4 22.7 %dynamic_update_slice.7 = f32[2,4096,512]{2,1,0:T(8,128)} dynamic-update-slice(f32[2,4096,512]{2,1,0:T(8,128)} %broadcast_in_dim.14, f32[2,2048,512]{2,1,0:T(8,128)} %pad_maximum_fusion.1, s32[]{:T(128)} %constant.59.clone.1, s32[]{:T(128)S(6)} %select_n.268, s32[]{:T(128)} %constant.59.clone.1) | dynamic-update-slice | bytes 16777220 | tf_op jit(solution)/shard_map/dynamic_update_slice | solution.py:151
  1062.1 152.7 %reduce-scatter.2.cloned.1.call-done = f32[2,1024,512]{2,1,0:T(8,128)} async-done(((f32[2,4096,512]{2,1,0:T(8,128)}), f32[2,1024,512]{2,1,0:T(8,128)}) %reduce-scatter.2.cloned.1.call-update) | async-done | bytes 4194320 | tf_op jit(solution)/shard_map/reduce_scatter | solution.py:152
  (89 shorter events, 156.0 us)
Async XLA Ops:
  6.5 93.9 %collective-permute-start = (f32[1,2,1024,512]{3,2,1,0:T(8,128)}, f32[1,2,1024,512]{3,2,1,0:T(8,128)}, u32[]{:S(2)}, u32[]{:S(2)}) collective-permute-start(f32[1,2,1024,512]{3,2,1,0:T(8,128)} %bitcast.197), channel_id=1, source_target_pairs={{0,8},{8,0},{16,24},{24,16},{1,9},{9,1},{17,25},{25,17},{2,10},{10... | collective-permute-start | bytes 12582920 | tf_op jit(solution)/shard_map/ppermute | solution.py:21
  104.9 4.8 copy-start
  104.9 5.8 copy-start.2
  104.9 7.5 copy-start.10
  104.9 9.5 copy-start.9
  110.7 181.9 %collective-permute-start.1 = (f32[2,2,1024,512]{3,2,1,0:T(8,128)}, f32[2,2,1024,512]{3,2,1,0:T(8,128)}, u32[]{:S(2)}, u32[]{:S(2)}) collective-permute-start(f32[2,2,1024,512]{3,2,1,0:T(8,128)} %pad_maximum_fusion), channel_id=1, source_target_pairs={{0,16},{8,24},{16,0},{24,8},{1,17},{9,25},{17,1},{25,9},{2,18},{10... | collective-permute-start | bytes 25165832 | tf_op jit(solution)/shard_map/ppermute | solution.py:21
  127.1 165.5 %copy-start.3 = (f32[1,2,1024,512]{3,2,1,0:T(8,128)S(1)}, f32[1,2,1024,512]{3,2,1,0:T(8,128)}, u32[]{:S(2)}) copy-start(f32[1,2,1024,512]{3,2,1,0:T(8,128)} %copy-done.2) | copy-start | bytes 12582916
  131.3 161.4 %copy-start.1 = (f32[1,2,1024,512]{3,2,1,0:T(8,128)S(1)}, f32[1,2,1024,512]{3,2,1,0:T(8,128)}, u32[]{:S(2)}) copy-start(f32[1,2,1024,512]{3,2,1,0:T(8,128)} %copy-done) | copy-start | bytes 12582916
  357.5 3.7 copy-start.7
  357.5 4.1 copy-start.8
  444.0 189.0 %all-to-all-start = ((f32[2,2048,512]{2,0,1:T(2,128)}), f32[2,2048,512]{2,0,1:T(2,128)}, u32[]{:S(2)}, u32[]{:S(2)}) async-start(f32[2,2048,512]{2,0,1:T(2,128)} %copy.155), calls=%async_computation | async-start | bytes 16777216 | tf_op jit(solution)/shard_map/all_to_all | solution.py:124
  659.8 9.7 copy-start.5
  681.0 3.1 copy-start.6
  685.9 9.1 copy-start.4
  722.4 188.8 %all-to-all-start.1 = ((f32[2,256,4096]{1,0,2:T(2,128)}), f32[2,256,4096]{1,0,2:T(2,128)}, u32[]{:S(2)}, u32[]{:S(2)}) async-start(f32[2,256,4096]{1,0,2:T(2,128)} %copy_dynamic-update-slice_fusion), calls=%async_computation.1 | async-start | bytes 16777216 | tf_op jit(solution)/shard_map/all_to_all | solution.py:144
  727.3 487.5 %reduce-scatter.2.cloned.1.call-start = ((), (), s32[]{:S(2)}) async-start(), calls=%async_computation.3 | async-start | bytes 20971520 | tf_op jit(solution)/shard_map/reduce_scatter | solution.py:152
Sparse Core Ops, SparseCore 0:
  1062.2 152.5 reduce-scatter.1
